TPU v7x, 256 devices: a whole 4x4x8 slice. The times are simulated.
256 devices in a mesh: req: 64 (over z, y, core), tp: 4 (over x).
Axes of the slice: x: 4, y: 4, z: 8, core: 2. Of those that a mesh axis runs over, the one named last changes fastest.
Arguments:
- hidden_in: bfloat16 [8192, 2048], P('req'), may hold values from -6 to 6
- attn_gain: float32 [2048], replicated, may hold values from 0.1 to 1.9
- w_query: bfloat16 [2048, 3072], P(None, 'tp'), may hold values from -0.125 to 0.125
- w_latent: bfloat16 [2048, 576], P(None, 'tp'), may hold values from -0.125 to 0.125
- kv_gain: float32 [512], replicated, may hold values from 0.1 to 1.9
- w_key_up: bfloat16 [512, 2048], P(None, 'tp'), may hold values from -0.25 to 0.25
- w_value_up: bfloat16 [512, 2048], P(None, 'tp'), may hold values from -0.25 to 0.25
- w_out: bfloat16 [2048, 2048], P('tp'), may hold values from -0.125 to 0.125
- moe_gain: float32 [2048], replicated, may hold values from 0.1 to 1.9
- w_gate: bfloat16 [64, 2048, 1408], P('req', None, 'tp'), may hold values from -0.125 to 0.125
- w_up: bfloat16 [64, 2048, 1408], P('req', None, 'tp'), may hold values from -0.125 to 0.125
- w_down: bfloat16 [64, 1408, 2048], P('req', 'tp'), may hold values from -0.15625 to 0.15625
- latent_cache: bfloat16 [2048, 64, 576], P('req'), may hold values from -3000 to 3000
- page_table: int32 [256, 8], P('req'), may hold values from 0 to 7, as said below
- cache_len: int32 [256], P('req'), may hold values from 1 to 512, 65536 in all
- parents: int32 [256, 3, 8], P('req'), may hold values from 0 to 7
- routes: int32 [8192, 6], P('req'), may hold values from 0 to 63, all different within a row; in each aligned block of 128 rows (0 to 127, 128 to 255, ...) at most 24 rows name the same one
- route_weights: float32 [8192, 6], P('req'), may hold values from 0.1 to 1
Outputs:
- layer_out: bfloat16 [8192, 2048], P('req', 'tp')
Inputs may be any that keep to these rules, and one draw needn't show every extreme that they name: `page_table`: each request's row lists the 8 pages of that request's block of the pool, each once. `routes`: each row names 6 different experts; in the rows of one index of req no expert is named more than 24 times, a bound that some block reaches.
All inputs are finite; a program needn't handle non-finite values. No bound on the sum of `cache_len` on one device may be relied on, other than what follows from the above.
Results may differ from a plain program's by a relative error of at most 0.015.
The roundings to bfloat16 on the way count: a program that leaves them out, or rounds other values in their place, can miss the bound.
Values may be sent and summed in bfloat16 or wider, within the bound.
No kernel may reach another device: no remote copies, remote signals or barrier semaphores. Data moves between devices by JAX's collectives and lax.ppermute only.
A program may use at most 128 MiB of HBM per device.

v0:
```python
import jax
import jax.numpy as jnp
from jax import lax
from jax.sharding import PartitionSpec as P

D = 2048
NOPE = 128
ROPE = 64
VDIM = 128
LATENT = 512
TOPK = 6
EXP_DEV = 1
BEAMS = 8
STEPS = 4
PAGE = 64
PAGES = 8
MOE_CHUNKS = 4
eps = 1e-06
rope_base = 50000.0


def rms_scale(values):
    return lax.rsqrt(jnp.mean(values * values, axis=-1, keepdims=True) + eps)


def rotate(values, cos_val, sin_val):
    half_rope = values.shape[-1] // 2
    first = values[..., :half_rope]
    second = values[..., half_rope:]
    return jnp.concatenate(
        [first * cos_val - second * sin_val, second * cos_val + first * sin_val], axis=-1
    )


def expert_math(arrived, gate_w, up_w, down_w):
    gate_val = jnp.einsum("nesd,edf->nesf", arrived, gate_w, preferred_element_type=jnp.float32)
    up_val = jnp.einsum("nesd,edf->nesf", arrived, up_w, preferred_element_type=jnp.float32)
    active = (jax.nn.silu(gate_val) * up_val).astype(jnp.bfloat16)
    return jnp.einsum("nesf,efd->nesd", active, down_w, preferred_element_type=jnp.float32)


def send_home(shares):
    return lax.all_to_all(shares, "req", split_axis=0, concat_axis=0, tiled=True)


def local(
    hidden_in,
    attn_gain,
    w_query,
    w_latent,
    kv_gain,
    w_key_up,
    w_value_up,
    w_out,
    moe_gain,
    w_gate,
    w_up,
    w_down,
    latent_cache,
    page_table,
    cache_len,
    parents,
    routes,
    route_weights,
):
    highest = lax.Precision.HIGHEST
    row_count = hidden_in.shape[0]
    req_local = cache_len.shape[0]
    heads_local = w_value_up.shape[1] // VDIM
    tp_count = lax.axis_size("tp")
    req_count = lax.axis_size("req")
    col_share = D // tp_count
    max_len = PAGES * PAGE
    hidden_f = hidden_in.astype(jnp.float32)
    normed = (hidden_f * rms_scale(hidden_f) * attn_gain).astype(jnp.bfloat16)
    positions = (
        cache_len.astype(jnp.float32)[:, None, None]
        + jnp.arange(STEPS, dtype=jnp.float32)[None, :, None]
        + jnp.zeros((1, 1, BEAMS), jnp.float32)
    ).reshape(row_count)
    frequency = rope_base ** (-2.0 * jnp.arange(ROPE // 2, dtype=jnp.float32) / ROPE)
    angles = positions[:, None] * frequency[None, :]
    cos_val = jnp.cos(angles)
    sin_val = jnp.sin(angles)
    queries = jnp.dot(normed, w_query, preferred_element_type=jnp.float32).reshape(
        row_count, heads_local, NOPE + ROPE
    )
    q_nope = queries[:, :, :NOPE].astype(jnp.bfloat16)
    q_rope = rotate(queries[:, :, NOPE:], cos_val[:, None, :], sin_val[:, None, :]).astype(
        jnp.bfloat16
    )
    kv_part = jnp.dot(normed, w_latent, preferred_element_type=jnp.float32)
    kv_all = lax.all_gather(kv_part, "tp", axis=1, tiled=True)
    new_lat = kv_all[:, :LATENT] * rms_scale(kv_all[:, :LATENT]) * kv_gain
    new_rope = rotate(kv_all[:, LATENT:], cos_val, sin_val)
    new_keys = jnp.concatenate([new_lat, new_rope], axis=1).astype(jnp.bfloat16)
    key_up = w_key_up.reshape(LATENT, heads_local, NOPE)
    q_lat = jnp.einsum("nhc,lhc->nhl", q_nope, key_up, preferred_element_type=jnp.float32).astype(
        jnp.bfloat16
    )
    query_key = jnp.concatenate([q_lat, q_rope], axis=2)
    pool_index = (jnp.arange(req_local, dtype=jnp.int32) * PAGES)[:, None] + page_table
    cache_keys = jnp.take(latent_cache, pool_index.reshape(-1), axis=0).reshape(
        req_local, max_len, LATENT + ROPE
    )
    live_mask = jnp.arange(max_len, dtype=jnp.int32)[None, :] < cache_len[:, None]
    score_scale = (NOPE + ROPE) ** (-0.5)
    grouped = query_key.reshape(req_local, STEPS * BEAMS * heads_local, LATENT + ROPE)
    s_cache = (
        jnp.einsum("rqd,rld->rql", grouped, cache_keys, preferred_element_type=jnp.float32)
        * score_scale
    )
    s_cache = jnp.where(live_mask[:, None, :], s_cache, -jnp.inf).reshape(
        req_local, STEPS, BEAMS, heads_local, max_len
    )
    fresh = new_keys.reshape(req_local, STEPS, BEAMS, LATENT + ROPE).astype(jnp.float32)
    parent_hot = (parents[..., None] == jnp.arange(BEAMS, dtype=jnp.int32)).astype(jnp.float32)
    identity = jnp.broadcast_to(jnp.eye(BEAMS, dtype=jnp.float32), (req_local, BEAMS, BEAMS))
    tail_rows = []
    for step_index in range(STEPS):
        lineage = identity
        pieces = [None] * STEPS
        for earlier in range(step_index, -1, -1):
            pieces[earlier] = jnp.einsum(
                "rba,rad->rbd", lineage, fresh[:, earlier], precision=highest
            )
            if earlier > 0:
                lineage = jnp.einsum(
                    "rba,rac->rbc", lineage, parent_hot[:, earlier - 1], precision=highest
                )
        for later in range(step_index + 1, STEPS):
            pieces[later] = jnp.zeros_like(pieces[0])
        tail_rows.append(jnp.stack(pieces, axis=2))
    tail_keys = jnp.stack(tail_rows, axis=1).astype(jnp.bfloat16)
    queries_tail = query_key.reshape(req_local, STEPS, BEAMS, heads_local, LATENT + ROPE)
    s_tail = (
        jnp.einsum(
            "rsbhd,rsbjd->rsbhj", queries_tail, tail_keys, preferred_element_type=jnp.float32
        )
        * score_scale
    )
    causal = jnp.arange(STEPS)[None, :] <= jnp.arange(STEPS)[:, None]
    s_tail = jnp.where(causal[None, :, None, None, :], s_tail, -jnp.inf)
    top_score = jnp.maximum(jnp.max(s_cache, axis=-1), jnp.max(s_tail, axis=-1))
    e_cache = jnp.exp(s_cache - top_score[..., None])
    e_tail = jnp.exp(s_tail - top_score[..., None])
    total = jnp.sum(e_cache, axis=-1) + jnp.sum(e_tail, axis=-1)
    p_cache = (e_cache / total[..., None]).astype(jnp.bfloat16)
    p_tail = (e_tail / total[..., None]).astype(jnp.bfloat16)
    context = jnp.einsum(
        "rsbhl,rld->rsbhd", p_cache, cache_keys[..., :LATENT], preferred_element_type=jnp.float32
    )
    context = context + jnp.einsum(
        "rsbhj,rsbjd->rsbhd", p_tail, tail_keys[..., :LATENT], preferred_element_type=jnp.float32
    )
    context = context.astype(jnp.bfloat16).reshape(row_count, heads_local, LATENT)
    value_up = w_value_up.reshape(LATENT, heads_local, VDIM)
    head_out = (
        jnp.einsum("nhl,lhv->nhv", context, value_up, preferred_element_type=jnp.float32)
        .astype(jnp.bfloat16)
        .reshape(row_count, heads_local * VDIM)
    )
    attn_part = jnp.dot(head_out, w_out, preferred_element_type=jnp.float32)
    expert_count = EXP_DEV * req_count
    capacity = min(row_count, 2 * row_count * TOPK // expert_count)
    slot_count = expert_count * capacity
    picks = routes.reshape(-1)
    pick_hot = (picks[:, None] == jnp.arange(expert_count, dtype=jnp.int32)[None, :]).astype(
        jnp.int32
    )
    before = jnp.cumsum(pick_hot, axis=0) - pick_hot
    ranks = jnp.sum(before * pick_hot, axis=1)
    slot_of = picks * capacity + ranks
    slot_hot = (slot_of[:, None] == jnp.arange(slot_count, dtype=jnp.int32)[None, :]).reshape(
        row_count, TOPK, slot_count
    )
    gather_rows = jnp.sum(slot_hot.astype(jnp.int32), axis=1).astype(jnp.bfloat16)
    weight_rows = jnp.sum(jnp.where(slot_hot, route_weights[:, :, None], 0.0), axis=1)
    tp_index = lax.axis_index("tp")
    col_start = tp_index * col_share
    attn_cols = lax.psum_scatter(attn_part, "tp", scatter_dimension=1, tiled=True)
    hidden_cols = lax.dynamic_slice_in_dim(hidden_f, col_start, col_share, 1)
    resid_cols = hidden_cols + attn_cols
    square_sum = lax.psum(jnp.sum(resid_cols * resid_cols, axis=-1, keepdims=True), "tp")
    moe_scale = lax.rsqrt(square_sum / D + eps)
    gain_cols = lax.dynamic_slice_in_dim(moe_gain, col_start, col_share, 0)
    moe_in_cols = (resid_cols * moe_scale * gain_cols).astype(jnp.bfloat16)
    placed = jnp.dot(gather_rows.T, moe_in_cols, preferred_element_type=jnp.float32).astype(
        jnp.bfloat16
    )
    placed = placed.reshape(req_count, EXP_DEV, capacity, col_share)
    chunk = capacity // MOE_CHUNKS
    returned_parts = []
    for chunk_index in range(MOE_CHUNKS):
        arrived_cols = lax.all_to_all(
            placed[:, :, chunk_index * chunk : (chunk_index + 1) * chunk],
            "req",
            split_axis=0,
            concat_axis=0,
            tiled=True,
        )
        arrived = lax.all_gather(arrived_cols, "tp", axis=3, tiled=True)
        partial_out = expert_math(arrived, w_gate, w_up, w_down)
        shares = lax.psum_scatter(
            partial_out.astype(jnp.bfloat16), "tp", scatter_dimension=3, tiled=True
        )
        returned_parts.append(send_home(shares))
    returned = jnp.concatenate(returned_parts, axis=2)
    combined = jnp.dot(
        weight_rows, returned.reshape(slot_count, col_share).astype(jnp.float32), precision=highest
    )
    return (resid_cols + combined).astype(jnp.bfloat16)


def solution(mesh):
    in_specs = (
        P("req", None),
        P(),
        P(None, "tp"),
        P(None, "tp"),
        P(),
        P(None, "tp"),
        P(None, "tp"),
        P("tp", None),
        P(),
        P("req", None, "tp"),
        P("req", None, "tp"),
        P("req", "tp", None),
        P("req", None, None),
        P("req", None),
        P("req"),
        P("req", None, None),
        P("req", None),
        P("req", None),
    )
    out_specs = P("req", "tp")
    return jax.shard_map(local, mesh=mesh, in_specs=in_specs, out_specs=out_specs, check_vma=False)
```

profile of v0, /device:TPU:1, one launch (start us, length us, event | category | flops | bytes accessed | tf_op | source)
XLA Modules:
  0.0 439.2 jit_solution(9429141945775908812)
XLA Ops:
  9.4 1.6 fusion.199
  11.0 11.2 %all_gather.15 = f32[128,576]{0,1:T(8,128)S(1)} all-gather(f32[128,144]{0,1:T(8,128)S(1)} %fusion.199), channel_id=1, replica_groups=mesh['req'=64,'tp'=4] {'tp'}, dimensions={1}, use_global_device_ids=true | all-gather | bytes 368640 | tf_op jit(solution)/shard_map/all_gather | solution.py:93
  43.3 1.7 copy.232
  45.0 1.7 copy.231
  53.7 2.2 reshape.335
  55.9 3.0 fusion.227
  59.0 4.2 gather_fusion
  63.2 2.1 bitcast_select_fusion
  65.3 2.0 fusion.226
  67.4 2.5 reshape.337
  69.9 1.5 exponential_reduce_fusion
  73.2 1.9 fusion.185
  75.1 2.1 fusion.35
  78.1 2.0 copy.230
  81.7 3.0 fusion.228
  85.0 2.2 convert_element_type.135
  87.6 1.8 reduce-window.6
  92.3 22.1 %reduce-scatter.6.cloned.1.call-done = f32[128,512]{1,0:T(8,128)} async-done(((f32[128,2048]{1,0:T(8,128)}), f32[128,512]{1,0:T(8,128)}) %reduce-scatter.6.cloned.1.call-update) | async-done | bytes 262160 | tf_op jit(solution)/shard_map/reduce_scatter | solution.py:181
  115.6 6.5 %psum.7 = f32[128,1]{0,1:T(1,128)S(1)} all-reduce(f32[128,1]{0,1:T(1,128)S(1)} %bitcast.433), channel_id=1, replica_groups=mesh['req'=64,'tp'=4] {'tp'}, use_global_device_ids=true, to_apply=%region_13.14 | all-reduce | flops 128 | bytes 1024 | tf_op jit(solution)/shard_map/psum | solution.py:184
  122.1 1.8 convolution_convert_fusion
  125.3 31.6 %all_to_all.40 = bf16[64,1,6,512]{3,2,1,0:T(8,128)(2,1)S(1)} all-to-all(bf16[64,1,6,512]{3,2,1,0:T(8,128)(2,1)S(1)} %get-tuple-element.10), channel_id=1, replica_groups=mesh['req'=64,'tp'=4] {'req'}, dimensions={0} | all-to-all | bytes 786432 | tf_op jit(solution)/shard_map/all_to_all | solution.py:195
  157.9 23.4 %all_to_all.41 = bf16[64,1,6,512]{3,2,1,0:T(8,128)(2,1)S(1)} all-to-all(bf16[64,1,6,512]{3,2,1,0:T(8,128)(2,1)} %get-tuple-element.11), channel_id=1, replica_groups=mesh['req'=64,'tp'=4] {'req'}, dimensions={0} | all-to-all | bytes 786432 | tf_op jit(solution)/shard_map/all_to_all | solution.py:195
  182.3 23.4 %all_to_all.42 = bf16[64,1,6,512]{3,2,1,0:T(8,128)(2,1)S(1)} all-to-all(bf16[64,1,6,512]{3,2,1,0:T(8,128)(2,1)} %get-tuple-element.12), channel_id=1, replica_groups=mesh['req'=64,'tp'=4] {'req'}, dimensions={0} | all-to-all | bytes 786432 | tf_op jit(solution)/shard_map/all_to_all | solution.py:195
  206.7 23.4 %all_to_all.43 = bf16[64,1,6,512]{3,2,1,0:T(8,128)(2,1)S(1)} all-to-all(bf16[64,1,6,512]{3,2,1,0:T(8,128)(2,1)} %get-tuple-element.9), channel_id=1, replica_groups=mesh['req'=64,'tp'=4] {'req'}, dimensions={0} | all-to-all | bytes 786432 | tf_op jit(solution)/shard_map/all_to_all | solution.py:195
  231.1 3.7 fusion.81
  234.8 5.5 %fusion.3 = bf16[64,1,6,2048]{3,0,2,1:T(8,128)(2,1)} fusion(bf16[1,352,2048]{2,1,0:T(8,128)(2,1)} %param.29, bf16[1,2048,352]{1,2,0:T(8,128)(2,1)} %param.28, bf16[64,1,6,2048]{3,0,2,1:T(8,128)(2,1)} %all-gather.11.cloned.1.call-done, f32[64,1,6,352]{3,0,2,1:T(8,128)} %fusion.81), kind=kOutput, calls=%fused_computation.13 | convolution fusion | flops 1108893696 | bytes 6569984 | tf_op jit(solution)/shard_map/nesf,efd->nesd/dot_general | solution.py:39
  240.5 3.7 fusion.66
  244.2 5.5 %fusion.2 = bf16[64,1,6,2048]{3,0,2,1:T(8,128)(2,1)} fusion(bf16[1,352,2048]{2,1,0:T(8,128)(2,1)} %param.29, bf16[1,2048,352]{1,2,0:T(8,128)(2,1)} %param.28, bf16[64,1,6,2048]{3,0,2,1:T(8,128)(2,1)} %all-gather.9.cloned.1.call-done, f32[64,1,6,352]{3,0,2,1:T(8,128)} %fusion.66), kind=kOutput, calls=%fused_computation.12 | convolution fusion | flops 1108893696 | bytes 6569984 | tf_op jit(solution)/shard_map/nesf,efd->nesd/dot_general | solution.py:39
  250.0 3.7 fusion.51
  253.7 5.5 %fusion.1 = bf16[64,1,6,2048]{3,0,2,1:T(8,128)(2,1)} fusion(bf16[1,352,2048]{2,1,0:T(8,128)(2,1)} %param.29, bf16[1,2048,352]{1,2,0:T(8,128)(2,1)} %param.28, bf16[64,1,6,2048]{3,0,2,1:T(8,128)(2,1)} %all-gather.7.cloned.1.call-done, f32[64,1,6,352]{3,0,2,1:T(8,128)} %fusion.51), kind=kOutput, calls=%fused_computation.11 | convolution fusion | flops 1108893696 | bytes 6569984 | tf_op jit(solution)/shard_map/nesf,efd->nesd/dot_general | solution.py:39
  259.3 15.5 %all-gather.5.cloned.1.call-done = bf16[64,1,6,2048]{3,0,2,1:T(8,128)(2,1)} async-done(((bf16[64,1,6,512]{3,0,2,1:T(8,128)(2,1)}), bf16[64,1,6,2048]{3,0,2,1:T(8,128)(2,1)}) %all-gather.5.cloned.1.call-update) | async-done | bytes 1572880 | tf_op jit(solution)/shard_map/all_gather | solution.py:202
  274.8 3.7 fusion.36
  278.5 5.5 %fusion = bf16[64,1,6,2048]{3,0,2,1:T(8,128)(2,1)} fusion(bf16[1,352,2048]{2,1,0:T(8,128)(2,1)} %param.29, bf16[1,2048,352]{1,2,0:T(8,128)(2,1)} %param.28, bf16[64,1,6,2048]{3,0,2,1:T(8,128)(2,1)} %all-gather.5.cloned.1.call-done, f32[64,1,6,352]{3,0,2,1:T(8,128)} %fusion.36), kind=kOutput, calls=%fused_computation.10 | convolution fusion | flops 1108893696 | bytes 6569984 | tf_op jit(solution)/shard_map/nesf,efd->nesd/dot_general | solution.py:39
  284.0 20.7 %reduce-scatter.14.cloned.1.call-done = bf16[64,1,6,512]{3,0,2,1:T(8,128)(2,1)} async-done(((bf16[64,1,6,2048]{3,0,2,1:T(8,128)(2,1)}), bf16[64,1,6,512]{3,0,2,1:T(8,128)(2,1)}) %reduce-scatter.14.cloned.1.call-update) | async-done | bytes 393232 | tf_op jit(solution)/shard_map/reduce_scatter | solution.py:204
  304.7 2.0 copy.218
  306.8 11.9 %all-to-all-start.7 = ((bf16[64,1,6,512]{3,2,1,0:T(8,128)(2,1)}), bf16[64,1,6,512]{3,2,1,0:T(8,128)(2,1)}, u32[]{:S(2)}, u32[]{:S(2)}) async-start(bf16[64,1,6,512]{3,2,1,0:T(8,128)(2,1)} %copy.218), calls=%async_computation.12 | async-start | bytes 1048576 | tf_op jit(solution)/shard_map/all_to_all | solution.py:43
  318.6 16.8 %reduce-scatter.12.cloned.1.call-done = bf16[64,1,6,512]{3,0,2,1:T(8,128)(2,1)} async-done(((bf16[64,1,6,2048]{3,0,2,1:T(8,128)(2,1)}), bf16[64,1,6,512]{3,0,2,1:T(8,128)(2,1)}) %reduce-scatter.12.cloned.1.call-update) | async-done | bytes 393232 | tf_op jit(solution)/shard_map/reduce_scatter | solution.py:204
  335.5 2.0 copy.215
  337.5 11.9 %all-to-all-start.5 = ((bf16[64,1,6,512]{3,2,1,0:T(8,128)(2,1)}), bf16[64,1,6,512]{3,2,1,0:T(8,128)(2,1)}, u32[]{:S(2)}, u32[]{:S(2)}) async-start(bf16[64,1,6,512]{3,2,1,0:T(8,128)(2,1)} %copy.215), calls=%async_computation.9 | async-start | bytes 1048576 | tf_op jit(solution)/shard_map/all_to_all | solution.py:43
  349.4 16.9 %reduce-scatter.10.cloned.1.call-done = bf16[64,1,6,512]{3,0,2,1:T(8,128)(2,1)} async-done(((bf16[64,1,6,2048]{3,0,2,1:T(8,128)(2,1)}), bf16[64,1,6,512]{3,0,2,1:T(8,128)(2,1)}) %reduce-scatter.10.cloned.1.call-update) | async-done | bytes 393232 | tf_op jit(solution)/shard_map/reduce_scatter | solution.py:204
  366.2 2.0 copy.212
  368.2 12.0 %all-to-all-start.3 = ((bf16[64,1,6,512]{3,2,1,0:T(8,128)(2,1)}), bf16[64,1,6,512]{3,2,1,0:T(8,128)(2,1)}, u32[]{:S(2)}, u32[]{:S(2)}) async-start(bf16[64,1,6,512]{3,2,1,0:T(8,128)(2,1)} %copy.212), calls=%async_computation.6 | async-start | bytes 1048576 | tf_op jit(solution)/shard_map/all_to_all | solution.py:43
  380.3 16.7 %reduce-scatter.8.cloned.1.call-done = bf16[64,1,6,512]{3,0,2,1:T(8,128)(2,1)} async-done(((bf16[64,1,6,2048]{3,0,2,1:T(8,128)(2,1)}), bf16[64,1,6,512]{3,0,2,1:T(8,128)(2,1)}) %reduce-scatter.8.cloned.1.call-update) | async-done | bytes 393232 | tf_op jit(solution)/shard_map/reduce_scatter | solution.py:204
  397.0 2.0 copy.209
  399.0 11.9 %all-to-all-start.1 = ((bf16[64,1,6,512]{3,2,1,0:T(8,128)(2,1)}), bf16[64,1,6,512]{3,2,1,0:T(8,128)(2,1)}, u32[]{:S(2)}, u32[]{:S(2)}) async-start(bf16[64,1,6,512]{3,2,1,0:T(8,128)(2,1)} %copy.209), calls=%async_computation.3 | async-start | bytes 1048576 | tf_op jit(solution)/shard_map/all_to_all | solution.py:43
  410.9 1.5 select_reduce_fusion
  412.5 16.1 %all-to-all-done.1 = bf16[64,1,6,512]{3,2,1,0:T(8,128)(2,1)} async-done(((bf16[64,1,6,512]{3,2,1,0:T(8,128)(2,1)}), bf16[64,1,6,512]{3,2,1,0:T(8,128)(2,1)}, u32[]{:S(2)}, u32[]{:S(2)}) %all-to-all-start.1) | async-done | bytes 393248 | tf_op jit(solution)/shard_map/all_to_all | solution.py:43
  428.5 2.6 pad_maximum_fusion
  (147 shorter events, 47.0 us)
Async XLA Ops:
  6.5 34.7 %copy-start = (bf16[2048,768]{1,0:T(8,128)(2,1)S(1)}, bf16[2048,768]{1,0:T(8,128)(2,1)}, u32[]{:S(2)}) copy-start(bf16[2048,768]{1,0:T(8,128)(2,1)} %param.20) | copy-start | bytes 9437188
  6.5 17.9 %copy-start.14 = (f32[512]{0:T(512)S(1)}, f32[512]{0:T(512)}, u32[]{:S(2)}) copy-start(f32[512]{0:T(512)} %param.22) | copy-start | bytes 6148
  6.5 107.9 %reduce-scatter.6.cloned.1.call-start = ((), (), s32[]{:S(2)}) async-start(), calls=%async_computation.13 | async-start | bytes 1310720 | tf_op jit(solution)/shard_map/reduce_scatter | solution.py:181
  9.3 14.2 %copy-start.15 = (f32[128]{0:T(128)}, f32[128]{0:T(128)S(1)}, u32[]{:S(2)}) copy-start(f32[128]{0:T(128)S(1)} %add_rsqrt_fusion.1) | copy-start | bytes 1540
  9.4 17.3 %copy-start.12 = (s32[4,3,8]{2,0,1:T(4,128)S(1)}, s32[4,3,8]{2,0,1:T(4,128)}, u32[]{:S(2)}) copy-start(s32[4,3,8]{2,0,1:T(4,128)} %param.33) | copy-start | bytes 1156
  38.4 2.8 copy-start.3
  38.4 2.8 copy-start.10
  38.4 2.8 copy-start.16
  39.5 0.8 copy-start.7
  51.4 0.8 copy-start.6
  52.3 3.6 copy-start.17
  59.0 4.2 copy-start.11
  63.2 2.1 copy-start.5
  63.2 2.1 copy-start.9
  65.3 2.0 copy-start.1
  73.2 2.0 copy-start.2
  84.7 2.4 copy-start.8
  84.7 146.4 %all-gather.11.cloned.1.call-start = ((), (), s32[]{:S(2)}) async-start(), calls=%async_computation.20 | async-start | bytes 1966080 | tf_op jit(solution)/shard_map/all_gather | solution.py:202
  157.8 82.6 %all-gather.9.cloned.1.call-start = ((), (), s32[]{:S(2)}) async-start(), calls=%async_computation.18 | async-start | bytes 1966080 | tf_op jit(solution)/shard_map/all_gather | solution.py:202
  182.2 67.8 %all-gather.7.cloned.1.call-start = ((), (), s32[]{:S(2)}) async-start(), calls=%async_computation.16 | async-start | bytes 1966080 | tf_op jit(solution)/shard_map/all_gather | solution.py:202
  206.6 68.1 %all-gather.5.cloned.1.call-start = ((), (), s32[]{:S(2)}) async-start(), calls=%async_computation.14 | async-start | bytes 1966080 | tf_op jit(solution)/shard_map/all_gather | solution.py:202
  231.1 73.7 %reduce-scatter.14.cloned.1.call-start = ((), (), s32[]{:S(2)}) async-start(), calls=%async_computation.21 | async-start | bytes 1966080 | tf_op jit(solution)/shard_map/reduce_scatter | solution.py:204
  240.4 95.1 %reduce-scatter.12.cloned.1.call-start = ((), (), s32[]{:S(2)}) async-start(), calls=%async_computation.19 | async-start | bytes 1966080 | tf_op jit(solution)/shard_map/reduce_scatter | solution.py:204
  249.7 116.5 %reduce-scatter.10.cloned.1.call-start = ((), (), s32[]{:S(2)}) async-start(), calls=%async_computation.17 | async-start | bytes 1966080 | tf_op jit(solution)/shard_map/reduce_scatter | solution.py:204
  259.2 137.8 %reduce-scatter.8.cloned.1.call-start = ((), (), s32[]{:S(2)}) async-start(), calls=%async_computation.15 | async-start | bytes 1966080 | tf_op jit(solution)/shard_map/reduce_scatter | solution.py:204
  306.8 30.7 %all-to-all-start.7 = ((bf16[64,1,6,512]{3,2,1,0:T(8,128)(2,1)}), bf16[64,1,6,512]{3,2,1,0:T(8,128)(2,1)}, u32[]{:S(2)}, u32[]{:S(2)}) async-start(bf16[64,1,6,512]{3,2,1,0:T(8,128)(2,1)} %copy.218), calls=%async_computation.12 | async-start | bytes 1048576 | tf_op jit(solution)/shard_map/all_to_all | solution.py:43
  337.5 30.8 %all-to-all-start.5 = ((bf16[64,1,6,512]{3,2,1,0:T(8,128)(2,1)}), bf16[64,1,6,512]{3,2,1,0:T(8,128)(2,1)}, u32[]{:S(2)}, u32[]{:S(2)}) async-start(bf16[64,1,6,512]{3,2,1,0:T(8,128)(2,1)} %copy.215), calls=%async_computation.9 | async-start | bytes 1048576 | tf_op jit(solution)/shard_map/all_to_all | solution.py:43
  368.2 42.7 %copy-start.13 = (f32[128,6]{0,1:T(8,128)S(1)}, f32[128,6]{0,1:T(8,128)}, u32[]{:S(2)}) copy-start(f32[128,6]{0,1:T(8,128)} %param.35) | copy-start | bytes 9220
  368.2 30.8 %all-to-all-start.3 = ((bf16[64,1,6,512]{3,2,1,0:T(8,128)(2,1)}), bf16[64,1,6,512]{3,2,1,0:T(8,128)(2,1)}, u32[]{:S(2)}, u32[]{:S(2)}) async-start(bf16[64,1,6,512]{3,2,1,0:T(8,128)(2,1)} %copy.212), calls=%async_computation.6 | async-start | bytes 1048576 | tf_op jit(solution)/shard_map/all_to_all | solution.py:43
  399.0 29.5 %all-to-all-start.1 = ((bf16[64,1,6,512]{3,2,1,0:T(8,128)(2,1)}), bf16[64,1,6,512]{3,2,1,0:T(8,128)(2,1)}, u32[]{:S(2)}, u32[]{:S(2)}) async-start(bf16[64,1,6,512]{3,2,1,0:T(8,128)(2,1)} %copy.209), calls=%async_computation.3 | async-start | bytes 1048576 | tf_op jit(solution)/shard_map/all_to_all | solution.py:43
  428.5 2.6 copy-start.4
Sparse Core Ops, SparseCore 0:
  84.9 29.5 reduce-scatter.5
  157.9 23.6 all-gather.10
  183.6 29.1 all-gather.8
  214.6 29.1 all-gather.6
  245.6 29.1 all-gather.4
  277.3 27.3 reduce-scatter.13
  307.5 27.9 reduce-scatter.11
  338.2 27.9 reduce-scatter.9
  369.0 27.9 reduce-scatter.7
where the time goes:
time: 441 us; the launch traced here: 439 us
  waiting for transfers between devices  125 us (28%)
  blocking collectives  120 us (27%)
  matrix products  65.8 us (15%)
  starting transfers between devices  48.4 us (11%)
  local copies, waits for them, and re-layouts  39.7 us (9%)
  other arithmetic  27 us (6%)
  between operations  13.7 us (3%)
    all_to_all x4, blocking collectives, local(): lax.all_to_all(placed[:, :, chunk_index * chunk:(chunk_index + 1) * chunk...  102 us
    reduce_scatter x4, waiting for transfers between devices, local(): lax.psum_scatter(partial_out.astype(jnp.bfloat16), 'tp', scatter_dimensio...  71.2 us
    all_to_all x4, starting transfers between devices, send_home(): lax.all_to_all(shares, 'req', split_axis=0, concat_axis=0, tiled=True)  47.7 us
    reduce_scatter x1, waiting for transfers between devices, local(): lax.psum_scatter(attn_part, 'tp', scatter_dimension=1, tiled=True)  22.1 us
    dot_general x4, matrix products, expert_math(): jnp.einsum('nesf,efd->nesd', active, down_w, preferred_element_type=jnp.f...  22 us
    all_to_all x4, waiting for transfers between devices, send_home(): lax.all_to_all(shares, 'req', split_axis=0, concat_axis=0, tiled=True)  16.1 us
    all_gather x4, waiting for transfers between devices, local(): arrived = lax.all_gather(arrived_cols, 'tp', axis=3, tiled=True)  15.6 us
    dot_general x4, matrix products, expert_math(): jnp.einsum('nesd,edf->nesf', arrived, gate_w, preferred_element_type=jnp....  14.8 us
  transfers between devices with their start and end apart: 13, of which 7 were waited for; matrix products, arithmetic and copies ran while one was open for 13% of the time, Pallas kernels for 0%

commit v1 on v0

--- a/solution.py
+++ b/solution.py
@@ -1,3 +1,4 @@
+import functools
 import jax
 import jax.numpy as jnp
 from jax import lax
@@ -17,6 +18,25 @@
 MOE_CHUNKS = 4
 eps = 1e-06
 rope_base = 50000.0
+
+
+def _trace_ways(inner_x, comm_axis):
+    count_all = jax.lax.axis_size(comm_axis)
+    bank = []
+    for idx in range(1, count_all):
+        bank.append((idx - 1, idx))
+    current_value = bank + [(count_all - 1, 0)]
+    formed = inner_x
+    arrivals = [formed]
+    for _ in range(count_all - 1):
+        formed = jax.lax.ppermute(formed, comm_axis, current_value)
+        arrivals += [formed]
+    front = jnp.concatenate([*reversed(arrivals)], 1)
+    low = jnp.roll(front, (jax.lax.axis_index(comm_axis) + 1) * formed.shape[1], 1)
+    return low
+
+
+group_pipes_here = functools.partial(_trace_ways, comm_axis="tp")
 
 
 def rms_scale(values):
@@ -90,7 +110,7 @@
         jnp.bfloat16
     )
     kv_part = jnp.dot(normed, w_latent, preferred_element_type=jnp.float32)
-    kv_all = lax.all_gather(kv_part, "tp", axis=1, tiled=True)
+    kv_all = group_pipes_here(kv_part)
     new_lat = kv_all[:, :LATENT] * rms_scale(kv_all[:, :LATENT]) * kv_gain
     new_rope = rotate(kv_all[:, LATENT:], cos_val, sin_val)
     new_keys = jnp.concatenate([new_lat, new_rope], axis=1).astype(jnp.bfloat16)

time: 441 us -> 438 us (level); the launches traced: 439 us -> 431 us
  waiting for transfers between devices: 125 us -> 140 us
  blocking collectives: 120 us -> 108 us
  matrix products: 65.8 us -> 56.9 us
  other arithmetic: 27 us -> 21.3 us
    all_gather x1 -> x0, blocking collectives: 11.2 us -> none  [local(): kv_all = lax.all_gather(kv_part, 'tp', axis=1, tiled=True)]
    ppermute x0 -> x3, waiting for transfers between devices: none -> 7.09 us  [_trace_ways(): formed = jax.lax.ppermute(formed, comm_axis, current_value)]
    all_gather x4, waiting for transfers between devices: 15.6 us -> 20.4 us  [local(): arrived = lax.all_gather(arrived_cols, 'tp', axis=3, tiled=True)]
  transfers between devices with their start and end apart: 13 -> 16, of which waited for: 7 -> 9; matrix products, arithmetic and copies ran while one was open for 13% -> 16% of each run, Pallas kernels for 0% -> 0%
where the time goes in v1:
time: 438 us; the launch traced here: 431 us
  waiting for transfers between devices  140 us (32%)
  blocking collectives  108 us (25%)
  matrix products  56.9 us (13%)
  starting transfers between devices  51.3 us (12%)
  local copies, waits for them, and re-layouts  40 us (9%)
  other arithmetic  21.3 us (5%)
  between operations  14.1 us (3%)
    all_to_all x4, blocking collectives, local(): lax.all_to_all(placed[:, :, chunk_index * chunk:(chunk_index + 1) * chunk...  102 us
    reduce_scatter x4, waiting for transfers between devices, local(): lax.psum_scatter(partial_out.astype(jnp.bfloat16), 'tp', scatter_dimensio...  72.9 us
    all_to_all x4, starting transfers between devices, send_home(): lax.all_to_all(shares, 'req', split_axis=0, concat_axis=0, tiled=True)  47.1 us
    reduce_scatter x1, waiting for transfers between devices, local(): lax.psum_scatter(attn_part, 'tp', scatter_dimension=1, tiled=True)  23 us
    all_gather x4, waiting for transfers between devices, local(): arrived = lax.all_gather(arrived_cols, 'tp', axis=3, tiled=True)  20.4 us
    dot_general x4, matrix products, expert_math(): jnp.einsum('nesf,efd->nesd', active, down_w, preferred_element_type=jnp.f...  19.5 us
    all_to_all x4, waiting for transfers between devices, send_home(): lax.all_to_all(shares, 'req', split_axis=0, concat_axis=0, tiled=True)  16.2 us
    dot_general x4, matrix products, expert_math(): jnp.einsum('nesd,edf->nesf', arrived, gate_w, preferred_element_type=jnp....  11.8 us
  transfers between devices with their start and end apart: 16, of which 9 were waited for; matrix products, arithmetic and copies ran while one was open for 16% of the time, Pallas kernels for 0%

profile of v1, /device:TPU:1, one launch (start us, length us, event | category | flops | bytes accessed | tf_op | source)
XLA Modules:
  0.0 431.3 jit_solution(14284850287529520054)
XLA Ops:
  8.0 1.6 fusion.199
  9.6 2.1 collective-permute-start
  15.5 2.5 fusion.200
  19.1 4.1 gather_fusion
  23.2 2.0 bitcast_select_fusion
  26.9 1.7 copy.231
  28.6 2.0 copy.230
  32.5 3.2 collective-permute-done.1
  36.6 3.9 collective-permute-done.2
  58.7 2.2 reshape.335
  60.9 3.0 fusion.227
  64.0 3.0 fusion.226
  67.2 2.5 reshape.337
  69.7 1.6 exponential_reduce_fusion
  73.0 1.7 fusion.185
  77.3 1.5 fusion.228
  79.9 1.8 reduce-window.6
  83.7 23.0 %reduce-scatter.6.cloned.1.call-done = f32[128,512]{1,0:T(8,128)} async-done(((f32[128,2048]{1,0:T(8,128)}), f32[128,512]{1,0:T(8,128)}) %reduce-scatter.6.cloned.1.call-update) | async-done | bytes 262160 | tf_op jit(solution)/shard_map/reduce_scatter | solution.py:201
  107.8 6.4 %psum.7 = f32[128,1]{0,1:T(1,128)S(1)} all-reduce(f32[128,1]{0,1:T(1,128)S(1)} %bitcast.437), channel_id=1, replica_groups=mesh['req'=64,'tp'=4] {'tp'}, use_global_device_ids=true, to_apply=%region_13.14 | all-reduce | flops 128 | bytes 1024 | tf_op jit(solution)/shard_map/psum | solution.py:204
  116.3 31.8 %all_to_all.40 = bf16[64,1,6,512]{3,2,1,0:T(8,128)(2,1)S(1)} all-to-all(bf16[64,1,6,512]{3,2,1,0:T(8,128)(2,1)S(1)} %get-tuple-element.10), channel_id=1, replica_groups=mesh['req'=64,'tp'=4] {'req'}, dimensions={0} | all-to-all | bytes 786432 | tf_op jit(solution)/shard_map/all_to_all | solution.py:215
  149.0 23.4 %all_to_all.41 = bf16[64,1,6,512]{3,2,1,0:T(8,128)(2,1)S(1)} all-to-all(bf16[64,1,6,512]{3,2,1,0:T(8,128)(2,1)S(1)} %copy-done.13), channel_id=1, replica_groups=mesh['req'=64,'tp'=4] {'req'}, dimensions={0} | all-to-all | bytes 786432 | tf_op jit(solution)/shard_map/all_to_all | solution.py:215
  173.3 23.2 %all_to_all.42 = bf16[64,1,6,512]{3,2,1,0:T(8,128)(2,1)S(1)} all-to-all(bf16[64,1,6,512]{3,2,1,0:T(8,128)(2,1)S(1)} %copy-done.12), channel_id=1, replica_groups=mesh['req'=64,'tp'=4] {'req'}, dimensions={0} | all-to-all | bytes 786432 | tf_op jit(solution)/shard_map/all_to_all | solution.py:215
  197.5 23.2 %all_to_all.43 = bf16[64,1,6,512]{3,2,1,0:T(8,128)(2,1)S(1)} all-to-all(bf16[64,1,6,512]{3,2,1,0:T(8,128)(2,1)S(1)} %get-tuple-element.9), channel_id=1, replica_groups=mesh['req'=64,'tp'=4] {'req'}, dimensions={0} | all-to-all | bytes 786432 | tf_op jit(solution)/shard_map/all_to_all | solution.py:215
  221.7 2.9 fusion.81
  224.7 4.9 %fusion.3 = bf16[64,1,6,2048]{3,0,2,1:T(8,128)(2,1)} fusion(bf16[1,352,2048]{2,1,0:T(8,128)(2,1)} %param.29, bf16[1,2048,352]{1,2,0:T(8,128)(2,1)} %param.28, bf16[64,1,6,2048]{3,0,2,1:T(8,128)(2,1)S(1)} %copy-done.34, f32[64,1,6,352]{3,0,2,1:T(8,128)S(1)} %fusion.81), kind=kOutput, calls=%fused_computation.13 | convolution fusion | flops 1108893696 | bytes 6569984 | tf_op jit(solution)/shard_map/nesf,efd->nesd/dot_general | solution.py:59
  229.6 3.0 fusion.66
  232.6 4.9 %fusion.2 = bf16[64,1,6,2048]{3,0,2,1:T(8,128)(2,1)} fusion(bf16[1,352,2048]{2,1,0:T(8,128)(2,1)} %param.29, bf16[1,2048,352]{1,2,0:T(8,128)(2,1)} %param.28, bf16[64,1,6,2048]{3,0,2,1:T(8,128)(2,1)S(1)} %copy-done.33, f32[64,1,6,352]{3,0,2,1:T(8,128)S(1)} %fusion.66), kind=kOutput, calls=%fused_computation.12 | convolution fusion | flops 1108893696 | bytes 6569984 | tf_op jit(solution)/shard_map/nesf,efd->nesd/dot_general | solution.py:59
  237.6 2.9 fusion.51
  240.6 4.9 %fusion.1 = bf16[64,1,6,2048]{3,0,2,1:T(8,128)(2,1)} fusion(bf16[1,352,2048]{2,1,0:T(8,128)(2,1)} %param.29, bf16[1,2048,352]{1,2,0:T(8,128)(2,1)} %param.28, bf16[64,1,6,2048]{3,0,2,1:T(8,128)(2,1)S(1)} %copy-done.32, f32[64,1,6,352]{3,0,2,1:T(8,128)S(1)} %fusion.51), kind=kOutput, calls=%fused_computation.11 | convolution fusion | flops 1108893696 | bytes 6569984 | tf_op jit(solution)/shard_map/nesf,efd->nesd/dot_general | solution.py:59
  245.5 20.3 %all-gather.5.cloned.1.call-done = bf16[64,1,6,2048]{3,0,2,1:T(8,128)(2,1)} async-done(((bf16[64,1,6,512]{3,0,2,1:T(8,128)(2,1)}), bf16[64,1,6,2048]{3,0,2,1:T(8,128)(2,1)}) %all-gather.5.cloned.1.call-update) | async-done | bytes 1572880 | tf_op jit(solution)/shard_map/all_gather | solution.py:222
  265.9 2.9 fusion.36
  268.8 4.9 %fusion = bf16[64,1,6,2048]{3,0,2,1:T(8,128)(2,1)} fusion(bf16[1,352,2048]{2,1,0:T(8,128)(2,1)} %param.29, bf16[1,2048,352]{1,2,0:T(8,128)(2,1)} %param.28, bf16[64,1,6,2048]{3,0,2,1:T(8,128)(2,1)S(1)} %copy-done.31, f32[64,1,6,352]{3,0,2,1:T(8,128)S(1)} %fusion.36), kind=kOutput, calls=%fused_computation.10 | convolution fusion | flops 1108893696 | bytes 6569984 | tf_op jit(solution)/shard_map/nesf,efd->nesd/dot_general | solution.py:59
  273.7 22.1 %reduce-scatter.14.cloned.1.call-done = bf16[64,1,6,512]{3,0,2,1:T(8,128)(2,1)} async-done(((bf16[64,1,6,2048]{3,0,2,1:T(8,128)(2,1)}), bf16[64,1,6,512]{3,0,2,1:T(8,128)(2,1)}) %reduce-scatter.14.cloned.1.call-update) | async-done | bytes 393232 | tf_op jit(solution)/shard_map/reduce_scatter | solution.py:224
  295.8 2.0 copy.218
  297.8 11.9 %all-to-all-start.7 = ((bf16[64,1,6,512]{3,2,1,0:T(8,128)(2,1)}), bf16[64,1,6,512]{3,2,1,0:T(8,128)(2,1)S(1)}, u32[]{:S(2)}, u32[]{:S(2)}) async-start(bf16[64,1,6,512]{3,2,1,0:T(8,128)(2,1)} %copy.218), calls=%async_computation.12 | async-start | bytes 1048576 | tf_op jit(solution)/shard_map/all_to_all | solution.py:63
  309.7 16.8 %reduce-scatter.12.cloned.1.call-done = bf16[64,1,6,512]{3,0,2,1:T(8,128)(2,1)} async-done(((bf16[64,1,6,2048]{3,0,2,1:T(8,128)(2,1)}), bf16[64,1,6,512]{3,0,2,1:T(8,128)(2,1)}) %reduce-scatter.12.cloned.1.call-update) | async-done | bytes 393232 | tf_op jit(solution)/shard_map/reduce_scatter | solution.py:224
  326.6 2.0 copy.215
  328.6 11.7 %all-to-all-start.5 = ((bf16[64,1,6,512]{3,2,1,0:T(8,128)(2,1)}), bf16[64,1,6,512]{3,2,1,0:T(8,128)(2,1)S(1)}, u32[]{:S(2)}, u32[]{:S(2)}) async-start(bf16[64,1,6,512]{3,2,1,0:T(8,128)(2,1)} %copy.215), calls=%async_computation.9 | async-start | bytes 1048576 | tf_op jit(solution)/shard_map/all_to_all | solution.py:63
  340.3 17.0 %reduce-scatter.10.cloned.1.call-done = bf16[64,1,6,512]{3,0,2,1:T(8,128)(2,1)} async-done(((bf16[64,1,6,2048]{3,0,2,1:T(8,128)(2,1)}), bf16[64,1,6,512]{3,0,2,1:T(8,128)(2,1)}) %reduce-scatter.10.cloned.1.call-update) | async-done | bytes 393232 | tf_op jit(solution)/shard_map/reduce_scatter | solution.py:224
  357.3 2.0 copy.212
  359.4 11.8 %all-to-all-start.3 = ((bf16[64,1,6,512]{3,2,1,0:T(8,128)(2,1)}), bf16[64,1,6,512]{3,2,1,0:T(8,128)(2,1)S(1)}, u32[]{:S(2)}, u32[]{:S(2)}) async-start(bf16[64,1,6,512]{3,2,1,0:T(8,128)(2,1)} %copy.212), calls=%async_computation.6 | async-start | bytes 1048576 | tf_op jit(solution)/shard_map/all_to_all | solution.py:63
  371.2 16.9 %reduce-scatter.8.cloned.1.call-done = bf16[64,1,6,512]{3,0,2,1:T(8,128)(2,1)} async-done(((bf16[64,1,6,2048]{3,0,2,1:T(8,128)(2,1)}), bf16[64,1,6,512]{3,0,2,1:T(8,128)(2,1)}) %reduce-scatter.8.cloned.1.call-update) | async-done | bytes 393232 | tf_op jit(solution)/shard_map/reduce_scatter | solution.py:224
  388.1 2.0 copy.209
  390.2 11.7 %all-to-all-start.1 = ((bf16[64,1,6,512]{3,2,1,0:T(8,128)(2,1)}), bf16[64,1,6,512]{3,2,1,0:T(8,128)(2,1)S(1)}, u32[]{:S(2)}, u32[]{:S(2)}) async-start(bf16[64,1,6,512]{3,2,1,0:T(8,128)(2,1)} %copy.209), calls=%async_computation.3 | async-start | bytes 1048576 | tf_op jit(solution)/shard_map/all_to_all | solution.py:63
  401.9 1.5 select_reduce_fusion
  403.4 16.2 %all-to-all-done.1 = bf16[64,1,6,512]{3,2,1,0:T(8,128)(2,1)S(1)} async-done(((bf16[64,1,6,512]{3,2,1,0:T(8,128)(2,1)}), bf16[64,1,6,512]{3,2,1,0:T(8,128)(2,1)S(1)}, u32[]{:S(2)}, u32[]{:S(2)}) %all-to-all-start.1) | async-done | bytes 393248 | tf_op jit(solution)/shard_map/all_to_all | solution.py:63
  420.4 2.7 pad_maximum_fusion
  423.1 1.5 fusion.138
  (197 shorter events, 44.1 us)
Async XLA Ops:
  6.5 9.0 %copy-start = (bf16[2048,768]{1,0:T(8,128)(2,1)S(1)}, bf16[2048,768]{1,0:T(8,128)(2,1)}, u32[]{:S(2)}) copy-start(bf16[2048,768]{1,0:T(8,128)(2,1)} %param.20) | copy-start | bytes 9437188
  6.5 9.0 %copy-start.26 = (f32[2048]{0:T(1024)S(1)}, f32[2048]{0:T(1024)}, u32[]{:S(2)}) copy-start(f32[2048]{0:T(1024)} %param.19) | copy-start | bytes 24580
  6.5 5.2 %copy-start.27 = (s32[4,3,8]{2,0,1:T(4,128)S(1)}, s32[4,3,8]{2,0,1:T(4,128)}, u32[]{:S(2)}) copy-start(s32[4,3,8]{2,0,1:T(4,128)} %param.33) | copy-start | bytes 1156
  6.5 6.3 %copy-start.30 = (s32[4]{0:T(128)S(1)}, s32[4]{0:T(128)}, u32[]{:S(2)}) copy-start(s32[4]{0:T(128)} %param.32) | copy-start | bytes 52
  6.5 7.0 %copy-start.29 = (s32[4,8]{1,0:T(4,128)S(1)}, s32[4,8]{1,0:T(4,128)}, u32[]{:S(2)}) copy-start(s32[4,8]{1,0:T(4,128)} %param.31) | copy-start | bytes 388
  6.5 100.2 %reduce-scatter.6.cloned.1.call-start = ((), (), s32[]{:S(2)}) async-start(), calls=%async_computation.13 | async-start | bytes 1310720 | tf_op jit(solution)/shard_map/reduce_scatter | solution.py:201
  9.6 21.6 %collective-permute-start = (f32[128,144]{0,1:T(8,128)S(1)}, f32[128,144]{0,1:T(8,128)S(1)}, u32[]{:S(2)}, u32[]{:S(2)}) collective-permute-start(f32[128,144]{0,1:T(8,128)S(1)} %fusion.199), channel_id=1, source_target_pairs={{0,1},{1,2},{2,3},{3,0},{4,5},{5,6},{6,7},{7,4},{8,9},{9,10},{10,1... | collective-permute-start | bytes 221192 | tf_op jit(solution)/shard_map/ppermute | solution.py:32
  11.8 1.0 copy-start.17
  12.0 6.0 %copy-start.20 = (f32[4,8,8]{2,1,0:T(8,128)}, f32[4,8,8]{2,1,0:T(8,128)S(1)}, u32[]{:S(2)}) copy-start(f32[4,8,8]{2,1,0:T(8,128)S(1)} %fusion.207) | copy-start | bytes 3076
  12.9 5.1 %copy-start.19 = (f32[4,8,8]{2,1,0:T(8,128)}, f32[4,8,8]{2,1,0:T(8,128)S(1)}, u32[]{:S(2)}) copy-start(f32[4,8,8]{2,1,0:T(8,128)S(1)} %fusion.205) | copy-start | bytes 3076
  14.8 3.3 copy-start.21
  15.5 3.2 copy-start.16
  31.3 4.4 %collective-permute-start.1 = (f32[128,144]{0,1:T(8,128)S(1)}, f32[128,144]{0,1:T(8,128)S(1)}, u32[]{:S(2)}, u32[]{:S(2)}) collective-permute-start(f32[128,144]{0,1:T(8,128)S(1)} %collective-permute-done), channel_id=1, source_target_pairs={{0,1},{1,2},{2,3},{3,0},{4,5},{5,6},{6,7},{7,4},{8,9},{9,10},{10,1... | collective-permute-start | bytes 221192 | tf_op jit(solution)/shard_map/ppermute | solution.py:32
  35.7 4.9 %collective-permute-start.2 = (f32[128,144]{0,1:T(8,128)S(1)}, f32[128,144]{0,1:T(8,128)S(1)}, u32[]{:S(2)}, u32[]{:S(2)}) collective-permute-start(f32[128,144]{0,1:T(8,128)S(1)} %collective-permute-done.1), channel_id=1, source_target_pairs={{0,1},{1,2},{2,3},{3,0},{4,5},{5,6},{6,7},{7,4},{8,9},{9,10},{10,1... | collective-permute-start | bytes 221192 | tf_op jit(solution)/shard_map/ppermute | solution.py:32
  40.6 6.6 %copy-start.18 = (f32[8,8]{1,0:T(8,128)S(1)}, f32[8,8]{1,0:T(8,128)}, u32[]{:S(2)}) copy-start(f32[8,8]{1,0:T(8,128)} %copy-done.17) | copy-start | bytes 772
  53.3 1.9 copy-start.22
  54.1 1.0 copy-start.23
  57.3 3.6 copy-start.35
  60.9 3.1 copy-start.25
  69.7 3.3 slice-start
  73.0 1.7 copy-start.14
  74.7 1.0 copy-start.11
  75.6 1.6 copy-start.10
  77.3 1.6 copy-start.2
  78.8 142.9 %all-gather.11.cloned.1.call-start = ((), (), s32[]{:S(2)}) async-start(), calls=%async_computation.20 | async-start | bytes 1966080 | tf_op jit(solution)/shard_map/all_gather | solution.py:222
  116.3 32.7 %copy-start.13 = (bf16[64,1,6,512]{3,2,1,0:T(8,128)(2,1)S(1)}, bf16[64,1,6,512]{3,2,1,0:T(8,128)(2,1)}, u32[]{:S(2)}) copy-start(bf16[64,1,6,512]{3,2,1,0:T(8,128)(2,1)} %get-tuple-element.11) | copy-start | bytes 1179652
  148.9 24.4 %copy-start.12 = (bf16[64,1,6,512]{3,2,1,0:T(8,128)(2,1)S(1)}, bf16[64,1,6,512]{3,2,1,0:T(8,128)(2,1)}, u32[]{:S(2)}) copy-start(bf16[64,1,6,512]{3,2,1,0:T(8,128)(2,1)} %get-tuple-element.12) | copy-start | bytes 1179652
  148.9 80.7 %all-gather.9.cloned.1.call-start = ((), (), s32[]{:S(2)}) async-start(), calls=%async_computation.18 | async-start | bytes 1966080 | tf_op jit(solution)/shard_map/all_gather | solution.py:222
  173.3 64.3 %all-gather.7.cloned.1.call-start = ((), (), s32[]{:S(2)}) async-start(), calls=%async_computation.16 | async-start | bytes 1966080 | tf_op jit(solution)/shard_map/all_gather | solution.py:222
  197.4 68.4 %all-gather.5.cloned.1.call-start = ((), (), s32[]{:S(2)}) async-start(), calls=%async_computation.14 | async-start | bytes 1966080 | tf_op jit(solution)/shard_map/all_gather | solution.py:222
  221.6 74.2 %reduce-scatter.14.cloned.1.call-start = ((), (), s32[]{:S(2)}) async-start(), calls=%async_computation.21 | async-start | bytes 1966080 | tf_op jit(solution)/shard_map/reduce_scatter | solution.py:224
  221.7 3.0 copy-start.34
  229.6 97.0 %reduce-scatter.12.cloned.1.call-start = ((), (), s32[]{:S(2)}) async-start(), calls=%async_computation.19 | async-start | bytes 1966080 | tf_op jit(solution)/shard_map/reduce_scatter | solution.py:224
  229.6 3.0 copy-start.33
  237.5 119.8 %reduce-scatter.10.cloned.1.call-start = ((), (), s32[]{:S(2)}) async-start(), calls=%async_computation.17 | async-start | bytes 1966080 | tf_op jit(solution)/shard_map/reduce_scatter | solution.py:224
  237.6 3.0 copy-start.32
  245.5 142.7 %reduce-scatter.8.cloned.1.call-start = ((), (), s32[]{:S(2)}) async-start(), calls=%async_computation.15 | async-start | bytes 1966080 | tf_op jit(solution)/shard_map/reduce_scatter | solution.py:224
  265.9 3.0 copy-start.31
  297.8 30.8 %all-to-all-start.7 = ((bf16[64,1,6,512]{3,2,1,0:T(8,128)(2,1)}), bf16[64,1,6,512]{3,2,1,0:T(8,128)(2,1)S(1)}, u32[]{:S(2)}, u32[]{:S(2)}) async-start(bf16[64,1,6,512]{3,2,1,0:T(8,128)(2,1)} %copy.218), calls=%async_computation.12 | async-start | bytes 1048576 | tf_op jit(solution)/shard_map/all_to_all | solution.py:63
  328.6 61.6 %copy-start.6 = (bf16[64,1,6,512]{3,2,1,0:T(8,128)(2,1)}, bf16[64,1,6,512]{3,2,1,0:T(8,128)(2,1)S(1)}, u32[]{:S(2)}) copy-start(bf16[64,1,6,512]{3,2,1,0:T(8,128)(2,1)S(1)} %all-to-all-done.7) | copy-start | bytes 1179652
  328.6 30.8 %all-to-all-start.5 = ((bf16[64,1,6,512]{3,2,1,0:T(8,128)(2,1)}), bf16[64,1,6,512]{3,2,1,0:T(8,128)(2,1)S(1)}, u32[]{:S(2)}, u32[]{:S(2)}) async-start(bf16[64,1,6,512]{3,2,1,0:T(8,128)(2,1)} %copy.215), calls=%async_computation.9 | async-start | bytes 1048576 | tf_op jit(solution)/shard_map/all_to_all | solution.py:63
  359.3 42.5 %copy-start.28 = (f32[128,6]{0,1:T(8,128)S(1)}, f32[128,6]{0,1:T(8,128)}, u32[]{:S(2)}) copy-start(f32[128,6]{0,1:T(8,128)} %param.35) | copy-start | bytes 9220
  359.4 44.0 %copy-start.7 = (bf16[64,1,6,512]{3,2,1,0:T(8,128)(2,1)}, bf16[64,1,6,512]{3,2,1,0:T(8,128)(2,1)S(1)}, u32[]{:S(2)}) copy-start(bf16[64,1,6,512]{3,2,1,0:T(8,128)(2,1)S(1)} %all-to-all-done.5) | copy-start | bytes 1179652
  359.4 30.8 %all-to-all-start.3 = ((bf16[64,1,6,512]{3,2,1,0:T(8,128)(2,1)}), bf16[64,1,6,512]{3,2,1,0:T(8,128)(2,1)S(1)}, u32[]{:S(2)}, u32[]{:S(2)}) async-start(bf16[64,1,6,512]{3,2,1,0:T(8,128)(2,1)} %copy.212), calls=%async_computation.6 | async-start | bytes 1048576 | tf_op jit(solution)/shard_map/all_to_all | solution.py:63
  390.2 29.4 %copy-start.8 = (bf16[64,1,6,512]{3,2,1,0:T(8,128)(2,1)}, bf16[64,1,6,512]{3,2,1,0:T(8,128)(2,1)S(1)}, u32[]{:S(2)}) copy-start(bf16[64,1,6,512]{3,2,1,0:T(8,128)(2,1)S(1)} %all-to-all-done.3) | copy-start | bytes 1179652
  390.2 29.4 %all-to-all-start.1 = ((bf16[64,1,6,512]{3,2,1,0:T(8,128)(2,1)}), bf16[64,1,6,512]{3,2,1,0:T(8,128)(2,1)S(1)}, u32[]{:S(2)}, u32[]{:S(2)}) async-start(bf16[64,1,6,512]{3,2,1,0:T(8,128)(2,1)} %copy.209), calls=%async_computation.3 | async-start | bytes 1048576 | tf_op jit(solution)/shard_map/all_to_all | solution.py:63
  420.4 2.7 copy-start.3
  420.4 4.2 copy-start.1
  (5 other events, 4.1 us)
Sparse Core Ops, SparseCore 0:
  78.9 27.7 reduce-scatter.5
  149.0 23.6 all-gather.10
  174.7 29.1 all-gather.8
  205.7 29.1 all-gather.6
  236.7 29.1 all-gather.4
  268.4 27.3 reduce-scatter.13
  298.5 27.9 reduce-scatter.11
  329.3 27.9 reduce-scatter.9
  360.1 28.0 reduce-scatter.7
